TPU v7x, 32 devices: a whole 2x2x4 slice. The times are simulated.
32 devices in a mesh: dp: 4 (over z), expert: 8 (over y, x, core).
Axes of the slice: x: 2, y: 2, z: 4, core: 2. Of those that a mesh axis runs over, the one named last changes fastest.
Arguments:
- hidden: bfloat16 [3072, 2880], P('expert', 'dp'), may hold values from -6 to 6
- segments: int32 [8, 384], P('expert'), may hold values from 0 to 3, never falling along the last dimension, each value on 1 to 192 neighbouring positions
- request_adapter: int32 [8, 4], P('expert'), may hold values from 0 to 7
- routes: int32 [8, 384, 4], P('expert', 'dp'), may hold values from 0 to 7, all different within a row; in each aligned block of 96 rows (0 to 95, 96 to 191, ..., all dimensions but the last counted through in order) at most 64 rows name the same one
- expert_gates: bfloat16 [8, 384, 4], P('expert', 'dp'), may hold values from 0.049804688 to 0.59765625
- attention_gain: float32 [2880], replicated, may hold values from 0.25 to 1.75
- joined_weight: bfloat16 [2880, 4, 640], P(None, 'dp'), may hold values from -0.109375 to 0.109375
- sinks: float32 [32], P('dp'), may hold values from 0 to 3
- attention_out_weight: bfloat16 [2048, 2880], P('dp'), may hold values from -0.125 to 0.125
- joined_down_maps: bfloat16 [2880, 128], replicated, may hold values from -0.109375 to 0.109375
- joined_up_maps: bfloat16 [128, 4, 640], P(None, 'dp'), may hold values from -0.375 to 0.375
- output_down_maps: bfloat16 [2048, 128], P('dp'), may hold values from -0.125 to 0.125
- output_up_maps: bfloat16 [128, 2880], P(None, 'dp'), may hold values from -0.75 to 0.75
- expert_norm_gain: float32 [2880], replicated, may hold values from 0.25 to 1.75
- expert_gate_weight: bfloat16 [8, 2880, 2880], P('expert', None, 'dp'), may hold values from -0.109375 to 0.109375
- expert_up_weight: bfloat16 [8, 2880, 2880], P('expert', None, 'dp'), may hold values from -0.109375 to 0.109375
- expert_down_weight: bfloat16 [8, 2880, 2880], P('expert', 'dp'), may hold values from -0.109375 to 0.109375
- closing_gain: float32 [2880], replicated, may hold values from 0.25 to 1.75
- vocabulary_weight: bfloat16 [2880, 25600], P(None, ('dp', 'expert')), may hold values from -0.109375 to 0.109375
Outputs:
- hidden_out: bfloat16 [3072, 2880], P('expert', 'dp')
- logits: float32 [32, 25600], P(None, ('dp', 'expert'))
Inputs may be any that keep to these rules, and one draw needn't show every extreme that they name: `segments`: in each column the ids do not fall; each of the 4 requests has 1 to 192 tokens, and one has exactly 192. `routes`: the 4 experts of a token differ. Within the rows of one device (96 consecutive tokens, aligned blocks) no expert is named more than 64 times, and in some blocks one expert is named exactly 64 times.
All inputs are finite; a program needn't handle non-finite values.
Results may differ from a plain program's by a relative error of at most 0.02.
Values may be sent and summed in bfloat16 or wider, within the bound.
No kernel may reach another device: no remote copies, remote signals or barrier semaphores. Data moves between devices by JAX's collectives and lax.ppermute only.
A program may use at most 128 MiB of HBM per device.

v0:
```python
import jax
import jax.numpy as jnp
from jax import lax
from jax.sharding import PartitionSpec as P

HEAD_SIZE = 64
QUERY_GROUP = 8
TOP = 4
ADAPTER_RANK = 16
REQS = 4
epsilon = 1e-05
theta_base = 150000.0
adapter_scale = 2.0
glu_alpha = 1.702


def rms_scale(values, gain_row):
    mean_square = jnp.mean(values * values, axis=-1, keepdims=True)
    return values * lax.rsqrt(mean_square + epsilon) * gain_row


def positions_of(segment_row):
    counter = jnp.arange(segment_row.shape[0], dtype=jnp.int32)
    starting = jnp.concatenate(
        [jnp.ones((1,), dtype=jnp.bool_), segment_row[1:] != segment_row[:-1]]
    )
    first_index = lax.cummax(jnp.where(starting, counter, 0), axis=0)
    return counter - first_index


def adapter_per_token(segment_row, adapter_row):
    hits = segment_row[:, None] == jnp.arange(adapter_row.shape[0], dtype=jnp.int32)[None, :]
    return jnp.sum(jnp.where(hits, adapter_row[None, :], 0), axis=1)


def rotate_heads(values, positions):
    head_dim = values.shape[-1]
    half_dim = head_dim // 2
    frequency = theta_base ** (-2.0 * jnp.arange(half_dim, dtype=jnp.float32) / head_dim)
    angles = positions.astype(jnp.float32)[:, None] * frequency[None, :]
    cosine = jnp.cos(angles)[:, None, :]
    sine_part = jnp.sin(angles)[:, None, :]
    first_half = values[..., :half_dim]
    second_half = values[..., half_dim:]
    return jnp.concatenate(
        [
            first_half * cosine - second_half * sine_part,
            second_half * cosine + first_half * sine_part,
        ],
        axis=-1,
    )


def attend_heads(queries, key_heads, value_heads, segment_row, sink_row):
    tokens_now, kv_now, group_now, head_dim = queries.shape
    scores = jnp.einsum(
        "tkgh,skh->kgts", queries, key_heads, preferred_element_type=jnp.float32
    ) * head_dim ** (-0.5)
    counter = jnp.arange(tokens_now, dtype=jnp.int32)
    allowed = (segment_row[:, None] == segment_row[None, :]) & (
        counter[None, :] <= counter[:, None]
    )
    weights = jnp.where(allowed[None, None], jnp.exp(scores), 0.0)
    totals = jnp.sum(weights, axis=-1, keepdims=True) + jnp.exp(sink_row).reshape(
        kv_now, group_now, 1, 1
    )
    probs = (weights / totals).astype(jnp.bfloat16)
    blended_hidden = jnp.einsum(
        "kgts,skh->tkgh", probs, value_heads, preferred_element_type=jnp.float32
    )
    return blended_hidden.astype(jnp.bfloat16).reshape(tokens_now, kv_now * group_now * head_dim)


def shards(
    hidden,
    segments,
    request_adapter,
    routes,
    expert_gates,
    attention_gain,
    joined_weight,
    sinks,
    attention_out_weight,
    joined_down_maps,
    joined_up_maps,
    output_down_maps,
    output_up_maps,
    expert_norm_gain,
    expert_gate_weight,
    expert_up_weight,
    expert_down_weight,
    closing_gain,
    vocabulary_weight,
):
    groups = lax.axis_size("dp")
    columns = lax.axis_size("expert")
    position_dp = lax.axis_index("dp")
    segment_row = segments[0]
    adapter_row = request_adapter[0]
    col_tokens = segment_row.shape[0]
    gathered_rows = lax.all_gather(hidden, "dp", axis=1, tiled=True)
    width = gathered_rows.shape[1]
    normalized_hidden = rms_scale(gathered_rows.astype(jnp.float32), attention_gain).astype(
        jnp.bfloat16
    )
    joined_projection = jnp.dot(
        normalized_hidden, joined_weight.reshape(width, -1), preferred_element_type=jnp.float32
    )
    reduced_every_adapter = joined_down_maps.shape[1]
    reduced_hidden = jnp.dot(
        normalized_hidden, joined_down_maps, preferred_element_type=jnp.float32
    ).astype(jnp.bfloat16)
    rank_owner = jnp.arange(reduced_every_adapter, dtype=jnp.int32) // ADAPTER_RANK
    adapter_mask = adapter_per_token(segment_row, adapter_row)[:, None] == rank_owner[None, :]
    selected_reduced = jnp.where(adapter_mask, reduced_hidden, jnp.zeros_like(reduced_hidden))
    joined_projection = joined_projection + adapter_scale * jnp.dot(
        selected_reduced,
        joined_up_maps.reshape(reduced_every_adapter, -1),
        preferred_element_type=jnp.float32,
    )
    kv_here = joined_weight.shape[1]
    joined_projection = joined_projection.reshape(col_tokens, kv_here, QUERY_GROUP + 2, HEAD_SIZE)
    positions = positions_of(segment_row)
    queries = rotate_heads(
        joined_projection[:, :, :QUERY_GROUP].reshape(col_tokens, kv_here * QUERY_GROUP, HEAD_SIZE),
        positions,
    )
    queries = queries.astype(jnp.bfloat16).reshape(col_tokens, kv_here, QUERY_GROUP, HEAD_SIZE)
    key_heads = rotate_heads(joined_projection[:, :, QUERY_GROUP], positions).astype(jnp.bfloat16)
    value_heads = joined_projection[:, :, QUERY_GROUP + 1].astype(jnp.bfloat16)
    blended_hidden = attend_heads(queries, key_heads, value_heads, segment_row, sinks)
    partial_out = jnp.dot(blended_hidden, attention_out_weight, preferred_element_type=jnp.float32)
    mine_out = lax.psum_scatter(
        partial_out.astype(jnp.bfloat16), "dp", scatter_dimension=1, tiled=True
    ).astype(jnp.float32)
    output_reduced = lax.psum(
        jnp.dot(blended_hidden, output_down_maps, preferred_element_type=jnp.float32).astype(
            jnp.bfloat16
        ),
        "dp",
    )
    selected_output = jnp.where(adapter_mask, output_reduced, jnp.zeros_like(output_reduced))
    adapter_delta = adapter_scale * jnp.dot(
        selected_output, output_up_maps, preferred_element_type=jnp.float32
    )
    resid = (hidden.astype(jnp.float32) + mine_out + adapter_delta).astype(jnp.bfloat16)
    column_full = lax.all_gather(resid, "dp", axis=1, tiled=True)
    moe_in = rms_scale(column_full.astype(jnp.float32), expert_norm_gain).astype(jnp.bfloat16)
    share = col_tokens // groups
    experts = expert_gate_weight.shape[0] * columns
    capacity = 4 * share * TOP // (3 * experts)
    col_capacity = groups * capacity
    route_col = lax.all_gather(routes[0], "dp", axis=0, tiled=True)
    gates_col = lax.all_gather(expert_gates[0], "dp", axis=0, tiled=True)
    route_flat = route_col.reshape(-1)
    one_hot = (route_flat[:, None] == jnp.arange(experts, dtype=jnp.int32)[None, :]).astype(
        jnp.int32
    )
    slot_rows = jnp.sum((jnp.cumsum(one_hot, axis=0) - one_hot) * one_hot, axis=1)
    target = route_flat * col_capacity + slot_rows
    source_rows = jnp.arange(route_flat.shape[0], dtype=jnp.int32) // TOP
    table = jnp.full((experts * col_capacity,), col_tokens, jnp.int32).at[target].set(source_rows)
    padded = jnp.concatenate([moe_in, jnp.zeros((1, width), jnp.bfloat16)], axis=0)
    outgoing = jnp.take(padded, table, axis=0).reshape(experts, col_capacity, width)
    gate_weight = expert_gate_weight[0]
    up_weight = expert_up_weight[0]
    down_weight = expert_down_weight[0]
    arrived = lax.all_to_all(outgoing, "expert", split_axis=0, concat_axis=0, tiled=True)
    rows_in = arrived.reshape(-1, width)
    gate_part = jnp.dot(rows_in, gate_weight, preferred_element_type=jnp.float32)
    up_part = jnp.dot(rows_in, up_weight, preferred_element_type=jnp.float32)
    activated = (gate_part * jax.nn.sigmoid(glu_alpha * gate_part) * (up_part + 1.0)).astype(
        jnp.bfloat16
    )
    shares_out = (
        jnp.dot(activated, down_weight, preferred_element_type=jnp.float32)
        .astype(jnp.bfloat16)
        .reshape(experts, col_capacity, width)
    )
    answers = lax.all_to_all(shares_out, "expert", split_axis=0, concat_axis=0, tiled=True)
    picked_out = jnp.take(answers.reshape(experts * col_capacity, width), target, axis=0).reshape(
        col_tokens, TOP, width
    )
    mixture = jnp.einsum("tk,tkd->td", gates_col, picked_out, preferred_element_type=jnp.float32)
    moe_part = lax.psum_scatter(mixture.astype(jnp.bfloat16), "dp", scatter_dimension=1, tiled=True)
    moe_rounded = moe_part.astype(jnp.float32).astype(jnp.bfloat16)
    hidden_out = (resid.astype(jnp.float32) + moe_rounded.astype(jnp.float32)).astype(jnp.bfloat16)
    counter = jnp.arange(col_tokens, dtype=jnp.int32)
    request_ids = jnp.arange(REQS, dtype=jnp.int32)
    last_index = jnp.max(
        jnp.where(segment_row[None, :] == request_ids[:, None], counter[None, :], -1), axis=1
    )
    chosen = jnp.take(hidden_out, jnp.clip(last_index, 0, col_tokens - 1), axis=0)
    spread_rows = lax.all_gather(chosen, ("dp", "expert"), axis=0, tiled=True)
    quarter = chosen.shape[1]
    tail_full = (
        spread_rows.reshape(groups, columns * REQS, quarter)
        .transpose(1, 0, 2)
        .reshape(columns * REQS, groups * quarter)
    )
    tail_rows = rms_scale(tail_full.astype(jnp.float32), closing_gain).astype(jnp.bfloat16)
    logits = jnp.dot(tail_rows, vocabulary_weight, preferred_element_type=jnp.float32)
    return (hidden_out, logits)


def solution(mesh):
    in_specs = (
        P("expert", "dp"),
        P("expert", None),
        P("expert", None),
        P("expert", "dp", None),
        P("expert", "dp", None),
        P(),
        P(None, "dp", None),
        P("dp"),
        P("dp", None),
        P(),
        P(None, "dp", None),
        P("dp", None),
        P(None, "dp"),
        P(),
        P("expert", None, "dp"),
        P("expert", None, "dp"),
        P("expert", "dp", None),
        P(),
        P(None, ("dp", "expert")),
    )
    out_specs = (P("expert", "dp"), P(None, ("dp", "expert")))
    return jax.shard_map(shards, mesh=mesh, in_specs=in_specs, out_specs=out_specs, check_vma=False)
```

profile of v0, /device:TPU:0, one launch (start us, length us, event | category | flops | bytes accessed | tf_op | source)
XLA Modules:
  0.0 773.1 jit_solution(7064949755682146424)
XLA Ops:
  7.2 0.7 all-gather.6.cloned.1.call-update
  8.0 0.8 reduce.7
  8.8 0.8 compare_reduce_fusion
  9.7 0.3 reduce-window.15
  10.1 0.7 exp.18
  10.9 0.9 select_reduce_fusion
  11.9 0.3 multiply_cosine_fusion
  12.3 48.1 %all-gather.6.cloned.1.call-done = bf16[384,2880]{0,1:T(8,128)(2,1)} async-done(((bf16[384,720]{0,1:T(8,128)(2,1)}), bf16[384,2880]{0,1:T(8,128)(2,1)}) %all-gather.6.cloned.1.call-update) | async-done | bytes 2211856 | tf_op jit(solution)/shard_map/all_gather | solution.py:101
  60.4 2.2 fusion
  62.6 5.9 fusion.14
  68.5 4.8 fusion.21
  73.3 2.5 copy.58
  75.8 1.2 slice_bitcast_fusion
  77.0 0.9 slice_bitcast_fusion.1
  77.9 0.3 fusion.63
  78.3 1.3 fusion.13
  79.6 2.3 fusion.23
  81.9 0.7 copy-done.4
  82.6 1.0 convolution_convert_fusion.2
  83.7 4.1 convolution_convert_fusion.1
  87.9 29.0 %all-reduce.3.cloned.1.call-done = bf16[384,128]{1,0:T(8,128)(2,1)} async-done(((bf16[384,128]{1,0:T(8,128)(2,1)}), bf16[384,128]{1,0:T(8,128)(2,1)}) %all-reduce.3.cloned.1.call-update) | async-done | bytes 98320 | tf_op jit(solution)/shard_map/psum | solution.py:136
  116.8 48.0 %reduce-scatter.3.cloned.1.call-done = bf16[384,720]{0,1:T(8,128)(2,1)} async-done(((bf16[384,2880]{0,1:T(8,128)(2,1)}), bf16[384,720]{0,1:T(8,128)(2,1)}) %reduce-scatter.3.cloned.1.call-update) | async-done | bytes 552976 | tf_op jit(solution)/shard_map/reduce_scatter | solution.py:133
  164.9 2.4 fusion.22
  167.5 14.5 %all-gather = s32[1,384,4]{2,1,0:T(8,128)S(1)} all-gather(s32[1,96,4]{2,1,0:T(8,128)S(1)} %copy.60), channel_id=2, replica_groups=mesh['dp'=4,'expert'=8] {'dp'}, dimensions={1}, use_global_device_ids=true | all-gather | bytes 7680 | tf_op jit(solution)/shard_map/all_gather | solution.py:153
  182.0 0.1 eq.94
  182.2 0.1 reshape.421
  182.3 2.3 reduce-window.19
  184.6 0.3 slice_reduce_fusion
  184.9 0.2 reduce-window.24
  185.1 0.2 mul.226
  185.4 6.2 scatter_custom_fusion
  191.7 23.9 %all-gather.8.cloned.1.call-done = bf16[384,2880]{0,1:T(8,128)(2,1)} async-done(((bf16[384,720]{0,1:T(8,128)(2,1)}), bf16[384,2880]{0,1:T(8,128)(2,1)}) %all-gather.8.cloned.1.call-update) | async-done | bytes 2211856 | tf_op jit(solution)/shard_map/all_gather | solution.py:147
  215.5 2.2 fusion.3
  217.7 2.2 fusion.5
  219.9 2.6 copy.76
  222.5 1.8 concatenate.31.clone
  224.3 12.0 %gather_fusion = bf16[2048,2880]{1,0:T(8,128)(2,1)} fusion(bf16[385,2880]{1,0:T(8,128)(2,1)S(1)} %concatenate.31.clone, s32[2048]{0:T(1024)S(1)} %fusion.67), kind=kCustom, calls=%fused_computation | custom fusion | bytes 23601152 | tf_op jit(solution)/shard_map/jit(_take)/gather | solution.py:164
  236.3 15.2 %copy.62 = bf16[8,256,2880]{1,2,0:T(8,128)(2,1)} copy(bf16[8,256,2880]{2,1,0:T(8,128)(2,1)} %bitcast.123) | data formatting | bytes 23592960 | tf_op jit(solution)/shard_map/jit(_take)/gather | solution.py:164
  251.5 6.5 broadcast_select_fusion
  258.0 134.2 %all_to_all.10 = bf16[8,256,2880]{1,2,0:T(8,128)(2,1)} all-to-all(bf16[8,256,2880]{1,2,0:T(8,128)(2,1)S(1)} %broadcast_select_fusion), channel_id=1, replica_groups=mesh['dp'=4,'expert'=8] {'expert'}, dimensions={0} | all-to-all | bytes 23592960 | tf_op jit(solution)/shard_map/all_to_all | solution.py:168
  392.2 16.3 %copy.63 = bf16[8,256,2880]{2,1,0:T(8,128)(2,1)} copy(bf16[8,256,2880]{1,2,0:T(8,128)(2,1)} %all_to_all.10) | data formatting | bytes 23592960 | tf_op jit(solution)/shard_map/all_to_all | solution.py:168
  408.4 15.1 %fusion.7 = f32[2048,720]{0,1:T(8,128)} fusion(bf16[2048,2880]{1,0:T(8,128)(2,1)} %bitcast.125, bf16[1,2880,720]{1,2,0:T(8,128)(2,1)} %param.34), kind=kOutput, calls=%fused_computation.22 | convolution fusion | flops 8493465600 | bytes 21841920 | tf_op jit(solution)/shard_map/dot_general | solution.py:171
  423.6 26.6 %convolution_convert_fusion = bf16[2048,2880]{0,1:T(8,128)(2,1)} fusion(bf16[1,720,2880]{2,1,0:T(8,128)(2,1)} %param.35, f32[2048,720]{0,1:T(8,128)} %fusion.7, bf16[2048,2880]{1,0:T(8,128)(2,1)} %bitcast.126, bf16[1,2880,720]{1,2,0:T(8,128)(2,1)} %param.33), kind=kOutput, calls=%fused_computation.7 | convolution fusion | flops 17004625920 | bytes 37785600 | tf_op jit(solution)/shard_map/dot_general | solution.py:176
  450.2 10.1 %copy.82 = bf16[360,8,8,256]{3,2,0,1:T(8,128)(2,1)} copy(bf16[360,8,8,256]{3,2,1,0:T(8,128)(2,1)} %bitcast.127) | data formatting | bytes 23592960 | tf_op jit(solution)/shard_map/reshape | solution.py:178
  460.3 5.5 all-to-all-start.1
  465.8 0.2 reduce_sum.69
  466.1 0.1 copy.66
  466.2 13.8 %all-gather.1 = bf16[1,384,4]{2,0,1:T(2,128)(2,1)S(1)} all-gather(bf16[1,96,4]{2,0,1:T(2,128)(2,1)S(1)} %copy.66), channel_id=3, replica_groups=mesh['dp'=4,'expert'=8] {'dp'}, dimensions={1}, use_global_device_ids=true | all-gather | bytes 3840 | tf_op jit(solution)/shard_map/all_gather | solution.py:154
  480.1 0.1 copy.75
  480.4 116.0 %all-to-all-done.1 = bf16[8,256,2880]{1,2,0:T(8,128)(2,1)} async-done(((bf16[8,256,2880]{1,2,0:T(8,128)(2,1)}), bf16[8,256,2880]{1,2,0:T(8,128)(2,1)}, u32[]{:S(2)}, u32[]{:S(2)}) %all-to-all-start.1) | async-done | bytes 11796512 | tf_op jit(solution)/shard_map/all_to_all | solution.py:180
  596.4 16.3 %copy.65 = bf16[8,256,2880]{2,1,0:T(8,128)(2,1)} copy(bf16[8,256,2880]{1,2,0:T(8,128)(2,1)} %all-to-all-done.1) | data formatting | bytes 23592960 | tf_op jit(solution)/shard_map/all_to_all | solution.py:180
  612.6 22.9 %gather_fusion.1 = bf16[1536,2880]{1,0:T(8,128)(2,1)} fusion(bf16[2048,2880]{1,0:T(8,128)(2,1)} %bitcast.122, s32[2048]{0:T(1024)S(1)} %pad_clamp_fusion), kind=kCustom, calls=%fused_computation.1 | custom fusion | bytes 17700864 | tf_op jit(solution)/shard_map/jit(_take)/gather | solution.py:181
  635.5 12.9 %gather.19 = bf16[384,4,2880]{2,1,0:T(4,128)(2,1)} reshape(bf16[1536,2880]{1,0:T(8,128)(2,1)} %gather_fusion.1) | data formatting | bytes 17694720 | tf_op jit(solution)/shard_map/jit(_take)/gather | solution.py:181
  648.4 20.9 %multiply_reduce_fusion = bf16[384,2880]{1,0:T(8,128)(2,1)S(1)} fusion(f32[384,4]{1,0:T(8,128)S(1)} %copy.75, bf16[384,4,2880]{2,1,0:T(4,128)(2,1)} %gather.19, pred[384,4]{1,0:T(8,128)(4,1)S(1)} %compare_and_fusion), kind=kLoop, calls=%fused_computation.4 | loop fusion | flops 16588800 | bytes 11066880
  669.4 2.5 copy.74
  672.1 43.0 %reduce-scatter.5.cloned.1.call-done = bf16[384,720]{0,1:T(8,128)(2,1)} async-done(((bf16[384,2880]{0,1:T(8,128)(2,1)}), bf16[384,720]{0,1:T(8,128)(2,1)}) %reduce-scatter.5.cloned.1.call-update) | async-done | bytes 552976 | tf_op jit(solution)/shard_map/reduce_scatter | solution.py:185
  715.1 2.1 add_convert_fusion
  717.3 1.3 copy.68
  718.6 0.6 gather_fusion.2
  719.2 40.3 %all-gather.2 = bf16[32,4,720]{2,1,0:T(4,128)(2,1)S(1)} all-gather(bf16[1,4,720]{2,1,0:T(4,128)(2,1)S(1)} %select_bitcast_fusion), channel_id=1, replica_groups=mesh['dp'=4,'expert'=8] {'dp','expert'}, dimensions={0}, use_global_device_ids=true | all-gather | bytes 190080 | tf_op jit(solution)/shard_map/all_gather | solution.py:194
  759.6 0.2 multiply_reduce_fusion.1
  759.8 1.0 copy.83
  760.8 1.2 reshape.426
  762.1 4.4 fusion.36
  (69 shorter events, 1.9 us)
Async XLA Ops:
  7.2 76.5 %copy-start = (bf16[512,2880]{0,1:T(8,128)(2,1)S(1)}, bf16[512,2880]{0,1:T(8,128)(2,1)}, u32[]{:S(2)}) copy-start(bf16[512,2880]{0,1:T(8,128)(2,1)} %param.27) | copy-start | bytes 8847364
  7.2 53.2 %all-gather.6.cloned.1.call-start = ((), (), s32[]{:S(2)}) async-start(), calls=%async_computation.4 | async-start | bytes 2764800 | tf_op jit(solution)/shard_map/all_gather | solution.py:101
  7.9 108.9 %all-reduce.3.cloned.1.call-start = ((), (), s32[]{:S(2)}) async-start(), calls=%async_computation.6 | async-start | bytes 196608 | tf_op jit(solution)/shard_map/psum | solution.py:136
  8.8 59.8 %copy-start.6 = (s32[384]{0:T(512)}, s32[384]{0:T(512)S(1)}, u32[]{:S(2)}) copy-start(s32[384]{0:T(512)S(1)} %reduce.7) | copy-start | bytes 4612
  62.6 6.0 copy-start.11
  62.6 6.0 copy-start.12
  79.6 3.0 copy-start.5
  81.9 0.8 copy-start.4
  83.6 81.3 %copy-start.3 = (bf16[384,720]{0,1:T(8,128)(2,1)S(1)}, bf16[384,720]{0,1:T(8,128)(2,1)}, u32[]{:S(2)}) copy-start(bf16[384,720]{0,1:T(8,128)(2,1)} %param.19) | copy-start | bytes 1658884
  83.6 81.3 %reduce-scatter.3.cloned.1.call-start = ((), (), s32[]{:S(2)}) async-start(), calls=%async_computation.5 | async-start | bytes 2764800 | tf_op jit(solution)/shard_map/reduce_scatter | solution.py:133
  87.8 79.6 %copy-start.9 = (s32[1,96,4]{1,2,0:T(4,128)S(1)}, s32[1,96,4]{1,2,0:T(4,128)}, u32[]{:S(2)}) copy-start(s32[1,96,4]{1,2,0:T(4,128)} %param.22) | copy-start | bytes 4612
  87.8 129.9 %copy-start.8 = (f32[2880]{0:T(1024)S(1)}, f32[2880]{0:T(1024)}, u32[]{:S(2)}) copy-start(f32[2880]{0:T(1024)} %param.32) | copy-start | bytes 34564
  87.8 127.7 %all-gather.8.cloned.1.call-start = ((), (), s32[]{:S(2)}) async-start(), calls=%async_computation.7 | async-start | bytes 2764800 | tf_op jit(solution)/shard_map/all_gather | solution.py:147
  460.3 5.7 copy-start.10
  460.3 136.1 %all-to-all-start.1 = ((bf16[8,256,2880]{1,2,0:T(8,128)(2,1)}), bf16[8,256,2880]{1,2,0:T(8,128)(2,1)}, u32[]{:S(2)}, u32[]{:S(2)}) async-start(bf16[8,256,2880]{1,2,0:T(8,128)(2,1)} %bitcast.124), calls=%async_computation.2 | async-start | bytes 23592960 | tf_op jit(solution)/shard_map/all_to_all | solution.py:180
  465.8 249.3 %reduce-scatter.5.cloned.1.call-start = ((), (), s32[]{:S(2)}) async-start(), calls=%async_computation.8 | async-start | bytes 2764800 | tf_op jit(solution)/shard_map/reduce_scatter | solution.py:185
  669.3 2.6 copy-start.7
  669.3 45.8 %copy-start.2 = (bf16[384,720]{0,1:T(8,128)(2,1)S(1)}, bf16[384,720]{0,1:T(8,128)(2,1)}, u32[]{:S(2)}) copy-start(bf16[384,720]{0,1:T(8,128)(2,1)} %fusion.22) | copy-start | bytes 1658884
  715.1 51.4 %copy-start.1 = (bf16[512,2880]{0,1:T(8,128)(2,1)S(1)}, bf16[512,2880]{0,1:T(8,128)(2,1)}, u32[]{:S(2)}) copy-start(bf16[512,2880]{0,1:T(8,128)(2,1)} %param.27) | copy-start | bytes 8847364
Sparse Core Ops, SparseCore 0:
  9.6 50.7 all-gather.5
  83.7 33.0 all-reduce.2
  119.3 45.5 reduce-scatter.2
  167.5 47.9 all-gather.7
  672.0 43.0 reduce-scatter.4
where the time goes:
time: 775 us; the launch traced here: 773 us
  waiting for transfers between devices  309 us (40%)
  blocking collectives  203 us (26%)
  local copies, waits for them, and re-layouts  131 us (17%)
  matrix products  67.9 us (9%)
  other arithmetic  43.1 us (6%)
  between operations  14.1 us (2%)
    all_to_all x1, blocking collectives, shards(): lax.all_to_all(outgoing, 'expert', split_axis=0, concat_axis=0, tiled=True)  134 us
    all_to_all x1, waiting for transfers between devices, shards(): lax.all_to_all(shares_out, 'expert', split_axis=0, concat_axis=0, tiled=T...  116 us
    all_gather x1, waiting for transfers between devices, shards(): gathered_rows = lax.all_gather(hidden, 'dp', axis=1, tiled=True)  48.1 us
    reduce_scatter x1, waiting for transfers between devices, shards(): lax.psum_scatter(partial_out.astype(jnp.bfloat16), 'dp', scatter_dimensio...  48 us
    reduce_scatter x1, waiting for transfers between devices, shards(): lax.psum_scatter(mixture.astype(jnp.bfloat16), 'dp', scatter_dimension=1,...  43 us
    all_gather x1, blocking collectives, shards(): spread_rows = lax.all_gather(chosen, ('dp', 'expert'), axis=0, tiled=True)  40.3 us
    gather x2, local copies, waits for them, and re-layouts, shards(): jnp.take(answers.reshape(experts * col_capacity, width), target, axis=0)  35.8 us
    psum x1, waiting for transfers between devices, shards(): lax.psum(jnp.dot(blended_hidden, output_down_maps, preferred_element_type...  29 us
  transfers between devices with their start and end apart: 6, of which 6 were waited for; matrix products, arithmetic and copies ran while one was open for 2% of the time, Pallas kernels for 0%

commit v1 on v0

--- a/solution.py
+++ b/solution.py
@@ -133,12 +133,12 @@
     mine_out = lax.psum_scatter(
         partial_out.astype(jnp.bfloat16), "dp", scatter_dimension=1, tiled=True
     ).astype(jnp.float32)
-    output_reduced = lax.psum(
+    output_reduced = lax.all_gather(
         jnp.dot(blended_hidden, output_down_maps, preferred_element_type=jnp.float32).astype(
             jnp.bfloat16
         ),
         "dp",
-    )
+    ).sum(axis=0)
     selected_output = jnp.where(adapter_mask, output_reduced, jnp.zeros_like(output_reduced))
     adapter_delta = adapter_scale * jnp.dot(
         selected_output, output_up_maps, preferred_element_type=jnp.float32

time: 775 us -> 745 us (0.961)
  waiting for transfers between devices: 309 us -> 262 us
  blocking collectives: 203 us -> 220 us
    psum x1 -> x0, waiting for transfers between devices: 29 us -> none  [shards(): lax.psum(jnp.dot(blended_hidden, output_down_maps, preferred_element_type...]
    reduce_scatter x1, waiting for transfers between devices: 48 us -> 29.5 us  [shards(): lax.psum_scatter(partial_out.astype(jnp.bfloat16), 'dp', scatter_dimensio...]
    all_gather x0 -> x1, blocking collectives: none -> 17.7 us  [shards(): lax.all_gather(jnp.dot(blended_hidden, output_down_maps, preferred_elemen...]
  transfers between devices with their start and end apart: 6 -> 5, of which waited for: 6 -> 5; matrix products, arithmetic and copies ran while one was open for 2% -> 2% of each run, Pallas kernels for 0% -> 0%
where the time goes in v1:
time: 745 us; the launch traced here: 743 us
  waiting for transfers between devices  262 us (35%)
  blocking collectives  220 us (30%)
  local copies, waits for them, and re-layouts  131 us (18%)
  matrix products  67.2 us (9%)
  other arithmetic  43.2 us (6%)
  between operations  14.1 us (2%)
    all_to_all x1, blocking collectives, shards(): lax.all_to_all(outgoing, 'expert', split_axis=0, concat_axis=0, tiled=True)  134 us
    all_to_all x1, waiting for transfers between devices, shards(): lax.all_to_all(shares_out, 'expert', split_axis=0, concat_axis=0, tiled=T...  116 us
    all_gather x1, waiting for transfers between devices, shards(): gathered_rows = lax.all_gather(hidden, 'dp', axis=1, tiled=True)  48.1 us
    reduce_scatter x1, waiting for transfers between devices, shards(): lax.psum_scatter(mixture.astype(jnp.bfloat16), 'dp', scatter_dimension=1,...  43 us
    all_gather x1, blocking collectives, shards(): spread_rows = lax.all_gather(chosen, ('dp', 'expert'), axis=0, tiled=True)  40.3 us
    gather x2, local copies, waits for them, and re-layouts, shards(): jnp.take(answers.reshape(experts * col_capacity, width), target, axis=0)  35.8 us
    reduce_scatter x1, waiting for transfers between devices, shards(): lax.psum_scatter(partial_out.astype(jnp.bfloat16), 'dp', scatter_dimensio...  29.5 us
    gather x2, local copies, waits for them, and re-layouts, shards(): jnp.take(padded, table, axis=0).reshape(experts, col_capacity, width)  27.2 us
  transfers between devices with their start and end apart: 5, of which 5 were waited for; matrix products, arithmetic and copies ran while one was open for 2% of the time, Pallas kernels for 0%

profile of v1, /device:TPU:0, one launch (start us, length us, event | category | flops | bytes accessed | tf_op | source)
XLA Modules:
  0.0 743.1 jit_solution(6430327750168231012)
XLA Ops:
  7.2 0.7 all-gather.7.cloned.1.call-update
  8.0 0.8 reduce.8
  8.8 0.8 compare_reduce_fusion
  9.7 0.3 reduce-window.15
  10.1 0.7 exp.18
  10.9 0.9 select_reduce_fusion
  11.9 0.3 multiply_cosine_fusion
  12.3 48.1 %all-gather.7.cloned.1.call-done = bf16[384,2880]{0,1:T(8,128)(2,1)} async-done(((bf16[384,720]{0,1:T(8,128)(2,1)}), bf16[384,2880]{0,1:T(8,128)(2,1)}) %all-gather.7.cloned.1.call-update) | async-done | bytes 2211856 | tf_op jit(solution)/shard_map/all_gather | solution.py:101
  60.4 2.2 fusion
  62.6 5.9 fusion.14
  68.5 4.8 fusion.21
  73.3 2.5 copy.58
  75.8 1.2 slice_bitcast_fusion
  77.0 0.9 slice_bitcast_fusion.1
  77.9 0.3 fusion.63
  78.3 1.3 fusion.13
  79.6 2.2 fusion.23
  81.8 0.7 copy-done.4
  82.6 3.1 convolution_convert_fusion.1
  85.8 1.3 convolution_convert_fusion.2
  87.1 17.7 %all-gather = bf16[1536,128]{1,0:T(8,128)(2,1)S(1)} all-gather(bf16[384,128]{1,0:T(8,128)(2,1)S(1)} %convolution_convert_fusion.2), channel_id=2, replica_groups=mesh['dp'=4,'expert'=8] {'dp'}, dimensions={0}, use_global_device_ids=true | all-gather | bytes 491520 | tf_op jit(solution)/shard_map/all_gather | solution.py:136
  104.8 29.5 %reduce-scatter.3.cloned.1.call-done = bf16[384,720]{0,1:T(8,128)(2,1)} async-done(((bf16[384,2880]{0,1:T(8,128)(2,1)}), bf16[384,720]{0,1:T(8,128)(2,1)}) %reduce-scatter.3.cloned.1.call-update) | async-done | bytes 552976 | tf_op jit(solution)/shard_map/reduce_scatter | solution.py:133
  134.3 2.4 fusion.22
  136.9 14.3 %all-gather.1 = s32[1,384,4]{2,1,0:T(8,128)S(1)} all-gather(s32[1,96,4]{2,1,0:T(8,128)S(1)} %copy.60), channel_id=3, replica_groups=mesh['dp'=4,'expert'=8] {'dp'}, dimensions={1}, use_global_device_ids=true | all-gather | bytes 7680 | tf_op jit(solution)/shard_map/all_gather | solution.py:153
  151.2 0.1 eq.94
  151.3 0.1 reshape.421
  151.5 2.3 reduce-window.19
  153.7 0.3 slice_reduce_fusion
  154.0 0.2 reduce-window.24
  154.2 0.2 mul.226
  154.5 6.2 scatter_custom_fusion
  160.8 24.9 %all-gather.9.cloned.1.call-done = bf16[384,2880]{0,1:T(8,128)(2,1)} async-done(((bf16[384,720]{0,1:T(8,128)(2,1)}), bf16[384,2880]{0,1:T(8,128)(2,1)}) %all-gather.9.cloned.1.call-update) | async-done | bytes 2211856 | tf_op jit(solution)/shard_map/all_gather | solution.py:147
  185.6 2.2 fusion.3
  187.8 2.2 fusion.5
  190.0 2.6 copy.76
  192.6 1.8 concatenate.31.clone
  194.4 12.0 %gather_fusion = bf16[2048,2880]{1,0:T(8,128)(2,1)} fusion(bf16[385,2880]{1,0:T(8,128)(2,1)S(1)} %concatenate.31.clone, s32[2048]{0:T(1024)S(1)} %fusion.67), kind=kCustom, calls=%fused_computation | custom fusion | bytes 23601152 | tf_op jit(solution)/shard_map/jit(_take)/gather | solution.py:164
  206.4 15.2 %copy.62 = bf16[8,256,2880]{1,2,0:T(8,128)(2,1)} copy(bf16[8,256,2880]{2,1,0:T(8,128)(2,1)} %bitcast.124) | data formatting | bytes 23592960 | tf_op jit(solution)/shard_map/jit(_take)/gather | solution.py:164
  221.6 6.5 broadcast_select_fusion
  228.1 134.2 %all_to_all.10 = bf16[8,256,2880]{1,2,0:T(8,128)(2,1)} all-to-all(bf16[8,256,2880]{1,2,0:T(8,128)(2,1)S(1)} %broadcast_select_fusion), channel_id=1, replica_groups=mesh['dp'=4,'expert'=8] {'expert'}, dimensions={0} | all-to-all | bytes 23592960 | tf_op jit(solution)/shard_map/all_to_all | solution.py:168
  362.3 16.3 %copy.63 = bf16[8,256,2880]{2,1,0:T(8,128)(2,1)} copy(bf16[8,256,2880]{1,2,0:T(8,128)(2,1)} %all_to_all.10) | data formatting | bytes 23592960 | tf_op jit(solution)/shard_map/all_to_all | solution.py:168
  378.6 15.1 %fusion.7 = f32[2048,720]{0,1:T(8,128)} fusion(bf16[2048,2880]{1,0:T(8,128)(2,1)} %bitcast.126, bf16[1,2880,720]{1,2,0:T(8,128)(2,1)} %param.34), kind=kOutput, calls=%fused_computation.22 | convolution fusion | flops 8493465600 | bytes 21841920 | tf_op jit(solution)/shard_map/dot_general | solution.py:171
  393.7 26.6 %convolution_convert_fusion = bf16[2048,2880]{0,1:T(8,128)(2,1)} fusion(bf16[1,720,2880]{2,1,0:T(8,128)(2,1)} %param.35, f32[2048,720]{0,1:T(8,128)} %fusion.7, bf16[2048,2880]{1,0:T(8,128)(2,1)} %bitcast.127, bf16[1,2880,720]{1,2,0:T(8,128)(2,1)} %param.33), kind=kOutput, calls=%fused_computation.7 | convolution fusion | flops 17004625920 | bytes 37785600 | tf_op jit(solution)/shard_map/dot_general | solution.py:176
  420.3 10.1 %copy.82 = bf16[360,8,8,256]{3,2,0,1:T(8,128)(2,1)} copy(bf16[360,8,8,256]{3,2,1,0:T(8,128)(2,1)} %bitcast.128) | data formatting | bytes 23592960 | tf_op jit(solution)/shard_map/reshape | solution.py:178
  430.4 5.5 all-to-all-start.1
  436.0 0.2 reduce_sum.82
  436.2 0.1 copy.66
  436.3 13.8 %all-gather.2 = bf16[1,384,4]{2,0,1:T(2,128)(2,1)S(1)} all-gather(bf16[1,96,4]{2,0,1:T(2,128)(2,1)S(1)} %copy.66), channel_id=4, replica_groups=mesh['dp'=4,'expert'=8] {'dp'}, dimensions={1}, use_global_device_ids=true | all-gather | bytes 3840 | tf_op jit(solution)/shard_map/all_gather | solution.py:154
  450.3 0.1 copy.75
  450.5 116.0 %all-to-all-done.1 = bf16[8,256,2880]{1,2,0:T(8,128)(2,1)} async-done(((bf16[8,256,2880]{1,2,0:T(8,128)(2,1)}), bf16[8,256,2880]{1,2,0:T(8,128)(2,1)}, u32[]{:S(2)}, u32[]{:S(2)}) %all-to-all-start.1) | async-done | bytes 11796512 | tf_op jit(solution)/shard_map/all_to_all | solution.py:180
  566.5 16.3 %copy.65 = bf16[8,256,2880]{2,1,0:T(8,128)(2,1)} copy(bf16[8,256,2880]{1,2,0:T(8,128)(2,1)} %all-to-all-done.1) | data formatting | bytes 23592960 | tf_op jit(solution)/shard_map/all_to_all | solution.py:180
  582.7 22.9 %gather_fusion.1 = bf16[1536,2880]{1,0:T(8,128)(2,1)} fusion(bf16[2048,2880]{1,0:T(8,128)(2,1)} %bitcast.123, s32[2048]{0:T(1024)S(1)} %pad_clamp_fusion), kind=kCustom, calls=%fused_computation.1 | custom fusion | bytes 17700864 | tf_op jit(solution)/shard_map/jit(_take)/gather | solution.py:181
  605.6 12.9 %gather.19 = bf16[384,4,2880]{2,1,0:T(4,128)(2,1)} reshape(bf16[1536,2880]{1,0:T(8,128)(2,1)} %gather_fusion.1) | data formatting | bytes 17694720 | tf_op jit(solution)/shard_map/jit(_take)/gather | solution.py:181
  618.5 20.9 %multiply_reduce_fusion = bf16[384,2880]{1,0:T(8,128)(2,1)S(1)} fusion(f32[384,4]{1,0:T(8,128)S(1)} %copy.75, bf16[384,4,2880]{2,1,0:T(4,128)(2,1)} %gather.19, pred[384,4]{1,0:T(8,128)(4,1)S(1)} %compare_and_fusion), kind=kLoop, calls=%fused_computation.4 | loop fusion | flops 16588800 | bytes 11066880
  639.5 2.5 copy.74
  642.2 43.0 %reduce-scatter.5.cloned.1.call-done = bf16[384,720]{0,1:T(8,128)(2,1)} async-done(((bf16[384,2880]{0,1:T(8,128)(2,1)}), bf16[384,720]{0,1:T(8,128)(2,1)}) %reduce-scatter.5.cloned.1.call-update) | async-done | bytes 552976 | tf_op jit(solution)/shard_map/reduce_scatter | solution.py:185
  685.2 2.1 add_convert_fusion
  687.3 1.3 copy.68
  688.6 0.6 gather_fusion.2
  689.3 40.3 %all-gather.3 = bf16[32,4,720]{2,1,0:T(4,128)(2,1)S(1)} all-gather(bf16[1,4,720]{2,1,0:T(4,128)(2,1)S(1)} %select_bitcast_fusion), channel_id=1, replica_groups=mesh['dp'=4,'expert'=8] {'dp','expert'}, dimensions={0}, use_global_device_ids=true | all-gather | bytes 190080 | tf_op jit(solution)/shard_map/all_gather | solution.py:194
  729.7 0.2 multiply_reduce_fusion.1
  729.9 1.0 copy.83
  730.8 1.2 reshape.426
  732.2 4.4 fusion.36
  (66 shorter events, 1.9 us)
Async XLA Ops:
  7.2 75.4 %copy-start = (bf16[512,2880]{0,1:T(8,128)(2,1)S(1)}, bf16[512,2880]{0,1:T(8,128)(2,1)}, u32[]{:S(2)}) copy-start(bf16[512,2880]{0,1:T(8,128)(2,1)} %param.27) | copy-start | bytes 8847364
  7.2 53.2 %all-gather.7.cloned.1.call-start = ((), (), s32[]{:S(2)}) async-start(), calls=%async_computation.4 | async-start | bytes 2764800 | tf_op jit(solution)/shard_map/all_gather | solution.py:101
  7.9 126.4 %reduce-scatter.3.cloned.1.call-start = ((), (), s32[]{:S(2)}) async-start(), calls=%async_computation.5 | async-start | bytes 2764800 | tf_op jit(solution)/shard_map/reduce_scatter | solution.py:133
  8.8 59.8 %copy-start.5 = (s32[384]{0:T(512)}, s32[384]{0:T(512)S(1)}, u32[]{:S(2)}) copy-start(s32[384]{0:T(512)S(1)} %reduce.8) | copy-start | bytes 4612
  62.6 6.0 copy-start.10
  62.6 6.0 copy-start.11
  81.8 0.8 copy-start.4
  82.6 51.7 %copy-start.3 = (bf16[384,720]{0,1:T(8,128)(2,1)S(1)}, bf16[384,720]{0,1:T(8,128)(2,1)}, u32[]{:S(2)}) copy-start(bf16[384,720]{0,1:T(8,128)(2,1)} %param.19) | copy-start | bytes 1658884
  85.7 51.1 %copy-start.8 = (s32[1,96,4]{1,2,0:T(4,128)S(1)}, s32[1,96,4]{1,2,0:T(4,128)}, u32[]{:S(2)}) copy-start(s32[1,96,4]{1,2,0:T(4,128)} %param.22) | copy-start | bytes 4612
  85.7 102.1 %copy-start.7 = (f32[2880]{0:T(1024)S(1)}, f32[2880]{0:T(1024)}, u32[]{:S(2)}) copy-start(f32[2880]{0:T(1024)} %param.32) | copy-start | bytes 34564
  85.7 99.9 %all-gather.9.cloned.1.call-start = ((), (), s32[]{:S(2)}) async-start(), calls=%async_computation.6 | async-start | bytes 2764800 | tf_op jit(solution)/shard_map/all_gather | solution.py:147
  430.4 5.7 copy-start.9
  430.4 136.1 %all-to-all-start.1 = ((bf16[8,256,2880]{1,2,0:T(8,128)(2,1)}), bf16[8,256,2880]{1,2,0:T(8,128)(2,1)}, u32[]{:S(2)}, u32[]{:S(2)}) async-start(bf16[8,256,2880]{1,2,0:T(8,128)(2,1)} %bitcast.125), calls=%async_computation.2 | async-start | bytes 23592960 | tf_op jit(solution)/shard_map/all_to_all | solution.py:180
  435.9 249.3 %reduce-scatter.5.cloned.1.call-start = ((), (), s32[]{:S(2)}) async-start(), calls=%async_computation.7 | async-start | bytes 2764800 | tf_op jit(solution)/shard_map/reduce_scatter | solution.py:185
  639.4 2.6 copy-start.6
  639.5 45.7 %copy-start.2 = (bf16[384,720]{0,1:T(8,128)(2,1)S(1)}, bf16[384,720]{0,1:T(8,128)(2,1)}, u32[]{:S(2)}) copy-start(bf16[384,720]{0,1:T(8,128)(2,1)} %fusion.22) | copy-start | bytes 1658884
  685.2 51.4 %copy-start.1 = (bf16[512,2880]{0,1:T(8,128)(2,1)S(1)}, bf16[512,2880]{0,1:T(8,128)(2,1)}, u32[]{:S(2)}) copy-start(bf16[512,2880]{0,1:T(8,128)(2,1)} %param.27) | copy-start | bytes 8847364
Sparse Core Ops, SparseCore 0:
  9.6 50.7 all-gather.6
  85.8 48.4 reduce-scatter.2
  136.9 48.7 all-gather.8
  642.1 42.9 reduce-scatter.4
